TPU v7x, 32 devices: a whole 2x2x4 slice. The times are simulated.
32 devices in a mesh: ctx: 4 (over x, core), ep: 8 (over z, y).
Axes of the slice: x: 2, y: 2, z: 4, core: 2. Of those that a mesh axis runs over, the one named last changes fastest.
Arguments:
- query_latent: bfloat16 [1, 512, 128, 512], P(None, 'ctx', 'ep'), may hold values from -6 to 6
- query_rope: bfloat16 [1, 128, 64, 512], P(None, 'ep', None, 'ctx'), may hold values from -12 to 12
- key_latent: bfloat16 [1, 512, 512], P(None, 'ctx'), may hold values from -6 to 6
- key_rope: bfloat16 [1, 64, 512], P(None, None, 'ctx'), may hold values from -14 to 14
- output_grad: bfloat16 [1, 512, 128, 512], P(None, 'ctx', 'ep'), may hold values from -6 to 6
Outputs:
- attended: bfloat16 [1, 512, 128, 512], P(None, 'ctx', 'ep')
- query_latent_grad: bfloat16 [1, 512, 128, 512], P(None, 'ctx', 'ep')
- query_rope_grad: bfloat16 [1, 128, 64, 512], P(None, 'ep', None, 'ctx')
- key_latent_grad: bfloat16 [1, 512, 512], P(None, 'ctx')
- key_rope_grad: bfloat16 [1, 64, 512], P(None, None, 'ctx')
All inputs are finite; a program needn't handle non-finite values.
Results may differ from a plain program's by a relative error of at most 0.018.
Values may be sent and summed in bfloat16 or wider, within the bound.
No kernel may reach another device: no remote copies, remote signals or barrier semaphores. Data moves between devices by JAX's collectives and lax.ppermute only.
A program may use at most 64 MiB of HBM per device.

v0:
```python
import jax
import jax.numpy as jnp
from jax import lax
from jax.sharding import PartitionSpec as P

scale_factor = 192.0 ** (-0.5)


def causal_reduce_ctx(blocks, n_ctx):
    here = lax.axis_index("ctx")
    total = jnp.take(blocks, here, axis=0).astype(jnp.float32)
    for shift in range(1, n_ctx):
        sent = jnp.take(blocks, jnp.maximum(here - shift, 0), axis=0)
        got = lax.ppermute(sent, "ctx", [(i, i - shift) for i in range(shift, n_ctx)])
        total = total + got.astype(jnp.float32)
    return total


def halving_sum_ep(total, n_ep):
    if n_ep & n_ep - 1:
        return lax.psum(total.astype(jnp.bfloat16), "ep").astype(jnp.bfloat16)
    n_bits = n_ep.bit_length() - 1
    here = lax.axis_index("ep")
    rows, cols = total.shape
    parts = total.reshape((2,) * n_bits + (rows // n_ep, cols))
    for k in range(n_bits):
        axis = n_bits - 1 - k
        mine = here >> k & 1
        keep = jnp.take(parts, mine, axis=axis)
        sent = jnp.take(parts, 1 - mine, axis=axis).astype(jnp.bfloat16)
        got = lax.ppermute(sent, "ep", [(i, i ^ 1 << k) for i in range(n_ep)])
        parts = keep + got.astype(jnp.float32)
        n_left = n_bits - 1 - k
        parts = parts.reshape((2,) * n_left + (rows // n_ep, cols)) if n_left else parts
    whole = parts.astype(jnp.bfloat16)
    for k in reversed(range(n_bits)):
        mine = here >> k & 1
        got = lax.ppermute(whole, "ep", [(i, i ^ 1 << k) for i in range(n_ep)])
        low = jnp.where(mine == 0, whole, got)
        high = jnp.where(mine == 0, got, whole)
        whole = jnp.stack([low, high], axis=n_bits - 1 - k)
    return whole.reshape(rows, cols)


def body(query_latent, query_rope, key_latent, key_rope, output_grad):
    n_ctx = lax.axis_size("ctx")
    n_ep = lax.axis_size("ep")
    block_len = query_latent.shape[1]
    kvr = key_latent.shape[2]
    local_keys = jnp.concatenate([key_latent[0], key_rope[0].T], axis=1)
    whole_keys = lax.all_gather(local_keys, "ctx", axis=0, tiled=True)
    whole_latent = whole_keys[None, :, :kvr]
    whole_rope = whole_keys[:, kvr:].T[None]
    length = whole_latent.shape[1]
    offset = lax.axis_index("ctx") * block_len
    query_place = offset + jnp.arange(block_len, dtype=jnp.int32)
    allowed = jnp.arange(length, dtype=jnp.int32)[None, :] <= query_place[:, None]
    scores = jnp.einsum(
        "sthd,sjd->shtj", query_latent, whole_latent, preferred_element_type=jnp.float32
    )
    scores = scores + jnp.einsum(
        "shdt,sdj->shtj", query_rope, whole_rope, preferred_element_type=jnp.float32
    )
    scores = jnp.where(allowed, scores * scale_factor, jnp.float32(-1e30))
    row_max = jnp.max(scores, axis=-1, keepdims=True)
    powers = jnp.exp(scores - row_max)
    weights = powers / jnp.sum(powers, axis=-1, keepdims=True)
    rounded_weights = weights.astype(jnp.bfloat16)
    attended = jnp.einsum(
        "shtj,sjd->sthd", rounded_weights, whole_latent, preferred_element_type=jnp.float32
    ).astype(jnp.bfloat16)
    row_dots = jnp.einsum(
        "sthd,sthd->sht", output_grad, attended, preferred_element_type=jnp.float32
    )
    weight_grad = jnp.einsum(
        "sthd,sjd->shtj", output_grad, whole_latent, preferred_element_type=jnp.float32
    )
    score_grad = (weights * (weight_grad - row_dots[..., None])).astype(jnp.bfloat16)
    latent_qgrad = (
        scale_factor
        * jnp.einsum("shtj,sjd->sthd", score_grad, whole_latent, preferred_element_type=jnp.float32)
    ).astype(jnp.bfloat16)
    rope_qgrad = (
        scale_factor
        * jnp.einsum("shtj,sdj->shdt", score_grad, whole_rope, preferred_element_type=jnp.float32)
    ).astype(jnp.bfloat16)
    latent_term = scale_factor * jnp.einsum(
        "shtj,sthd->jd", score_grad, query_latent, preferred_element_type=jnp.float32
    )
    latent_term = latent_term + jnp.einsum(
        "shtj,sthd->jd", rounded_weights, output_grad, preferred_element_type=jnp.float32
    )
    rope_term = scale_factor * jnp.einsum(
        "shtj,shdt->jd", score_grad, query_rope, preferred_element_type=jnp.float32
    )
    terms = jnp.concatenate([latent_term, rope_term], axis=1).astype(jnp.bfloat16)
    total = causal_reduce_ctx(terms.reshape(n_ctx, block_len, -1), n_ctx)
    total = halving_sum_ep(total, n_ep)
    latent_kgrad = total[None, :, :kvr]
    rope_kgrad = total[:, kvr:].T[None]
    return (attended, latent_qgrad, rope_qgrad, latent_kgrad, rope_kgrad)


def solution(mesh):
    placed = (
        P(None, "ctx", "ep", None),
        P(None, "ep", None, "ctx"),
        P(None, "ctx", None),
        P(None, None, "ctx"),
        P(None, "ctx", "ep", None),
    )
    return jax.shard_map(
        body,
        mesh=mesh,
        in_specs=placed,
        out_specs=(
            P(None, "ctx", "ep", None),
            P(None, "ctx", "ep", None),
            P(None, "ep", None, "ctx"),
            P(None, "ctx", None),
            P(None, None, "ctx"),
        ),
        check_vma=False,
    )
```

profile of v0, /device:TPU:0, one launch (start us, length us, event | category | flops | bytes accessed | tf_op | source)
XLA Modules:
  0.0 101.1 jit_solution(4417357890290526066)
XLA Ops:
  2.6 9.3 %all_gather.3 = bf16[512,576]{1,0:T(8,128)(2,1)S(1)} all-gather(bf16[128,576]{1,0:T(8,128)(2,1)S(1)} %pad_maximum_fusion), channel_id=1, replica_groups=mesh['ctx'=4,'ep'=8] {'ctx'}, dimensions={0}, use_global_device_ids=true | all-gather | bytes 737280 | tf_op jit(solution)/shard_map/all_gather | solution.py:51
  12.0 2.8 %fusion.23 = f32[512,128,16]{1,0,2:T(8,128)S(1)} fusion(bf16[128,16,512]{2,1,0:T(8,128)(2,1)S(1)} %bitcast.189, bf16[512,576]{1,0:T(8,128)(2,1)S(1)} %all_gather.3), kind=kOutput, calls=%fused_computation.27 | convolution fusion | flops 1073741824 | bytes 6815744 | tf_op jit(solution)/shard_map/sthd,sjd->shtj/dot_general | solution.py:58
  16.3 4.1 %bitcast_convert_fusion = (f32[16,128,512]{1,2,0:T(8,128)}, bf16[512,16,128]{2,0,1:T(8,128)(2,1)}) fusion(f32[16,128]{1,0:T(8,128)S(1)} %fusion.5, f32[1,16,128,512]{2,3,1,0:T(8,128)S(1)} %get-tuple-element.78, f32[16,128]{1,0:T(8,128)S(1)} %get-tuple-element.77, bf16[512,576]{1,0:T(8,128)(2,1)S(1)} %all_gather.3), kind=kOutput, calls=%fused_computation.18 | convolution fusion | flops 1078984704 | bytes 11026432 | tf_op jit(solution)/shard_map/shtj,sjd->sthd/dot_general | solution.py:69
  20.4 5.5 %copy.81 = f32[16,128,512]{2,0,1:T(8,128)} copy(f32[16,128,512]{1,2,0:T(8,128)} %get-tuple-element.79) | data formatting | bytes 8388608
  25.9 3.3 %multiply_reduce_fusion = f32[16,128]{0,1:T(8,128)S(1)} fusion(f32[16,128,512]{2,0,1:T(8,128)} %copy.81, bf16[1,128,16,512]{3,2,1,0:T(8,128)(2,1)} %param.17), kind=kLoop, calls=%fused_computation.6 | loop fusion | flops 3143680 | bytes 6299648
  29.3 6.8 %fusion.28 = f32[512,512]{1,0:T(8,128)} fusion(bf16[128,16,512]{2,1,0:T(8,128)(2,1)} %bitcast.191, f32[16,128]{1,0:T(8,128)S(1)} %fusion.5, f32[1,16,128,512]{2,3,1,0:T(8,128)} %copy-done.1, f32[16,128]{1,0:T(8,128)S(1)} %get-tuple-element.77), kind=kOutput, calls=%fused_computation.30 | convolution fusion | flops 1076887552 | bytes 7356416 | tf_op jit(solution)/shard_map/shtj,sthd->jd/dot_general | solution.py:90
  36.1 4.7 %fusion.1 = bf16[1,16,128,512]{2,3,1,0:T(8,128)(2,1)} fusion(f32[16,128]{1,0:T(8,128)S(1)} %copy.82, bf16[128,16,512]{2,1,0:T(8,128)(2,1)S(1)} %bitcast.192, f32[16,128]{1,0:T(8,128)S(1)} %fusion.5, f32[1,16,128,512]{2,3,1,0:T(8,128)S(1)} %copy-done.2, f32[16,128]{1,0:T(8,128)S(1)} %get-tuple-element.77, bf16[512,576]{1,0:T(8,128)(2,1)S(1)} %all_gather.3), kind=kOutput, calls=%fused_computation.2 | convolution fusion | flops 1078984704 | bytes 8937472 | tf_op jit(solution)/shard_map/sthd,sjd->shtj/dot_general | solution.py:75
  40.8 2.3 %fusion.69 = bf16[512,64]{0,1:T(8,128)(2,1)S(1)} fusion(bf16[1,16,128,512]{2,3,1,0:T(8,128)(2,1)} %fusion.1, bf16[1,16,64,128]{3,2,1,0:T(8,128)(2,1)S(1)} %copy-done.4), kind=kOutput, calls=%fused_computation.45 | convolution fusion | flops 134283264 | bytes 2424832 | tf_op jit(solution)/shard_map/shtj,shdt->jd/dot_general | solution.py:93
  43.1 4.4 %fusion.48 = bf16[512,512]{1,0:T(8,128)(2,1)S(1)} fusion(f32[512,512]{1,0:T(8,128)} %fusion.28, bf16[128,16,512]{2,1,0:T(8,128)(2,1)S(1)} %bitcast.190, bf16[1,16,128,512]{2,3,1,0:T(8,128)(2,1)} %fusion.1), kind=kOutput, calls=%fused_computation.34 | convolution fusion | flops 1074528256 | bytes 5767168 | tf_op jit(solution)/shard_map/shtj,sthd->jd/dot_general | solution.py:87
  52.7 2.8 %collective-permute-done.2 = bf16[128,576]{1,0:T(8,128)(2,1)} collective-permute-done((bf16[128,576]{1,0:T(8,128)(2,1)}, bf16[128,576]{1,0:T(8,128)(2,1)}, u32[]{:S(2)}, u32[]{:S(2)}) %collective-permute-start.2) | collective-permute-done | bytes 147488 | tf_op jit(solution)/shard_map/ppermute | solution.py:14
  55.5 3.6 %collective-permute-done.1 = bf16[128,576]{1,0:T(8,128)(2,1)} collective-permute-done((bf16[128,576]{1,0:T(8,128)(2,1)}, bf16[128,576]{1,0:T(8,128)(2,1)}, u32[]{:S(2)}, u32[]{:S(2)}) %collective-permute-start.1) | collective-permute-done | bytes 147488 | tf_op jit(solution)/shard_map/ppermute | solution.py:14
  61.0 1.6 %collective-permute-start.3 = (bf16[2,2,16,576]{3,2,1,0:T(8,128)(2,1)S(1)}, bf16[2,2,16,576]{3,2,1,0:T(8,128)(2,1)S(1)}, u32[]{:S(2)}, u32[]{:S(2)}) collective-permute-start(bf16[2,2,16,576]{3,2,1,0:T(8,128)(2,1)S(1)} %bitcast_convert_fusion.1), channel_id=1, source_target_pairs={{0,1},{1,0},{2,3},{3,2},{4,5},{5,4},{6,7},{7,6},{8,9},{9,8},{10,11... | collective-permute-start | bytes 221192 | tf_op jit(solution)/shard_map/ppermute | solution.py:31
  62.6 3.2 %collective-permute-done.3 = bf16[2,2,16,576]{3,2,1,0:T(8,128)(2,1)S(1)} collective-permute-done((bf16[2,2,16,576]{3,2,1,0:T(8,128)(2,1)S(1)}, bf16[2,2,16,576]{3,2,1,0:T(8,128)(2,1)S(1)}, u32[]{:S(2)}, u32[]{:S(2)}) %collective-permute-start.3) | collective-permute-done | bytes 73760 | tf_op jit(solution)/shard_map/ppermute | solution.py:31
  66.7 1.6 %collective-permute-start.4 = (bf16[2,16,576]{2,1,0:T(8,128)(2,1)S(1)}, bf16[2,16,576]{2,1,0:T(8,128)(2,1)S(1)}, u32[]{:S(2)}, u32[]{:S(2)}) collective-permute-start(bf16[2,16,576]{2,1,0:T(8,128)(2,1)S(1)} %bitcast_convert_fusion.2), channel_id=1, source_target_pairs={{0,2},{1,3},{2,0},{3,1},{4,6},{5,7},{6,4},{7,5},{8,10},{9,11},{10,... | collective-permute-start | bytes 110600 | tf_op jit(solution)/shard_map/ppermute | solution.py:31
  68.3 2.4 %collective-permute-done.4 = bf16[2,16,576]{2,1,0:T(8,128)(2,1)S(1)} collective-permute-done((bf16[2,16,576]{2,1,0:T(8,128)(2,1)S(1)}, bf16[2,16,576]{2,1,0:T(8,128)(2,1)S(1)}, u32[]{:S(2)}, u32[]{:S(2)}) %collective-permute-start.4) | collective-permute-done | bytes 36896 | tf_op jit(solution)/shard_map/ppermute | solution.py:31
  70.8 2.7 %collective-permute-start.5 = (bf16[16,576]{1,0:T(8,128)(2,1)S(1)}, bf16[16,576]{1,0:T(8,128)(2,1)S(1)}, u32[]{:S(2)}, u32[]{:S(2)}) collective-permute-start(bf16[16,576]{1,0:T(8,128)(2,1)S(1)} %bitcast_convert_fusion.3), channel_id=1, source_target_pairs={{0,4},{1,5},{2,6},{3,7},{4,0},{5,1},{6,2},{7,3},{8,12},{9,13},{10,... | collective-permute-start | bytes 55304 | tf_op jit(solution)/shard_map/ppermute | solution.py:31
  73.5 2.1 %collective-permute-done.5 = bf16[16,576]{1,0:T(8,128)(2,1)S(1)} collective-permute-done((bf16[16,576]{1,0:T(8,128)(2,1)S(1)}, bf16[16,576]{1,0:T(8,128)(2,1)S(1)}, u32[]{:S(2)}, u32[]{:S(2)}) %collective-permute-start.5) | collective-permute-done | bytes 18464 | tf_op jit(solution)/shard_map/ppermute | solution.py:31
  75.6 2.7 %collective-permute-start.6 = (bf16[16,576]{1,0:T(8,128)(2,1)S(1)}, bf16[16,576]{1,0:T(8,128)(2,1)S(1)}, u32[]{:S(2)}, u32[]{:S(2)}) collective-permute-start(bf16[16,576]{1,0:T(8,128)(2,1)S(1)} %fusion.90), channel_id=1, source_target_pairs={{0,4},{1,5},{2,6},{3,7},{4,0},{5,1},{6,2},{7,3},{8,12},{9,13},{10,... | collective-permute-start | bytes 55304 | tf_op jit(solution)/shard_map/ppermute | solution.py:38
  78.2 2.2 %collective-permute-done.6 = bf16[16,576]{1,0:T(8,128)(2,1)S(1)} collective-permute-done((bf16[16,576]{1,0:T(8,128)(2,1)S(1)}, bf16[16,576]{1,0:T(8,128)(2,1)S(1)}, u32[]{:S(2)}, u32[]{:S(2)}) %collective-permute-start.6) | collective-permute-done | bytes 18464 | tf_op jit(solution)/shard_map/ppermute | solution.py:38
  82.0 4.2 %fusion.25 = bf16[1,128,16,512]{1,3,2,0:T(8,128)(2,1)} fusion(bf16[1,16,128,512]{2,3,1,0:T(8,128)(2,1)} %fusion.1, bf16[512,576]{1,0:T(8,128)(2,1)S(1)} %all_gather.3), kind=kOutput, calls=%fused_computation.29 | convolution fusion | flops 1075838976 | bytes 4718592 | tf_op jit(solution)/shard_map/shtj,sjd->sthd/dot_general | solution.py:81
  86.2 1.6 %collective-permute-start.8 = (bf16[2,2,16,576]{3,2,0,1:T(8,128)(2,1)S(1)}, bf16[2,2,16,576]{3,2,0,1:T(8,128)(2,1)S(1)}, u32[]{:S(2)}, u32[]{:S(2)}) collective-permute-start(bf16[2,2,16,576]{3,2,0,1:T(8,128)(2,1)S(1)} %pad_maximum_fusion.2), channel_id=1, source_target_pairs={{0,1},{1,0},{2,3},{3,2},{4,5},{5,4},{6,7},{7,6},{8,9},{9,8},{10,11... | collective-permute-start | bytes 221192 | tf_op jit(solution)/shard_map/ppermute | solution.py:38
  87.8 2.8 %fusion.60 = bf16[1,16,64,128]{3,2,1,0:T(8,128)(2,1)} fusion(bf16[1,16,128,512]{2,3,1,0:T(8,128)(2,1)} %fusion.1, bf16[512,576]{1,0:T(8,128)(2,1)S(1)} %all_gather.3), kind=kOutput, calls=%fused_computation.42 | convolution fusion | flops 134479872 | bytes 2490368 | tf_op jit(solution)/shard_map/shtj,sdj->shdt/dot_general | solution.py:85
  90.6 4.5 %copy.70 = bf16[1,128,16,512]{3,2,1,0:T(8,128)(2,1)} copy(bf16[1,128,16,512]{1,3,2,0:T(8,128)(2,1)} %bitcast.193) | data formatting | bytes 4194304
  95.1 4.5 %copy.71 = bf16[1,128,16,512]{3,2,1,0:T(8,128)(2,1)} copy(bf16[1,128,16,512]{1,3,2,0:T(8,128)(2,1)} %fusion.25) | data formatting | bytes 4194304
  (45 shorter events, 14.5 us)
Async XLA Ops:
  0.6 11.3 %copy-start = (bf16[1,128,16,512]{3,2,1,0:T(8,128)(2,1)S(1)}, bf16[1,128,16,512]{3,2,1,0:T(8,128)(2,1)}, u32[]{:S(2)}) copy-start(bf16[1,128,16,512]{3,2,1,0:T(8,128)(2,1)} %param.13) | copy-start | bytes 6291460
  12.0 2.8 %copy-start.4 = (bf16[1,16,64,128]{3,2,1,0:T(8,128)(2,1)S(1)}, bf16[1,16,64,128]{3,2,1,0:T(8,128)(2,1)}, u32[]{:S(2)}) copy-start(bf16[1,16,64,128]{3,2,1,0:T(8,128)(2,1)} %param.14) | copy-start | bytes 786436
  15.7 4.7 %copy-start.1 = (f32[1,16,128,512]{2,3,1,0:T(8,128)}, f32[1,16,128,512]{2,3,1,0:T(8,128)S(1)}, u32[]{:S(2)}) copy-start(f32[1,16,128,512]{2,3,1,0:T(8,128)S(1)} %get-tuple-element.78) | copy-start | bytes 12582916
  29.3 6.8 %copy-start.2 = (f32[1,16,128,512]{2,3,1,0:T(8,128)S(1)}, f32[1,16,128,512]{2,3,1,0:T(8,128)}, u32[]{:S(2)}) copy-start(f32[1,16,128,512]{2,3,1,0:T(8,128)} %copy-done.1) | copy-start | bytes 12582916
  29.3 6.8 %copy-start.3 = (bf16[1,128,16,512]{3,2,1,0:T(8,128)(2,1)S(1)}, bf16[1,128,16,512]{3,2,1,0:T(8,128)(2,1)}, u32[]{:S(2)}) copy-start(bf16[1,128,16,512]{3,2,1,0:T(8,128)(2,1)} %param.17) | copy-start | bytes 6291460
  48.5 6.9 %collective-permute-start.2 = (bf16[128,576]{1,0:T(8,128)(2,1)}, bf16[128,576]{1,0:T(8,128)(2,1)}, u32[]{:S(2)}, u32[]{:S(2)}) collective-permute-start(bf16[128,576]{1,0:T(8,128)(2,1)} %get-tuple-element.70), channel_id=1, source_target_pairs={{24,0},{25,1},{26,2},{27,3},{28,4},{29,5},{30,6},{31,7}} | collective-permute-start | bytes 442376 | tf_op jit(solution)/shard_map/ppermute | solution.py:14
  49.8 9.2 %collective-permute-start.1 = (bf16[128,576]{1,0:T(8,128)(2,1)}, bf16[128,576]{1,0:T(8,128)(2,1)}, u32[]{:S(2)}, u32[]{:S(2)}) collective-permute-start(bf16[128,576]{1,0:T(8,128)(2,1)} %get-tuple-element.69), channel_id=1, source_target_pairs={{16,0},{24,8},{17,1},{25,9},{18,2},{26,10},{19,3},{27,11},{20,4},{... | collective-permute-start | bytes 442376 | tf_op jit(solution)/shard_map/ppermute | solution.py:14
  51.1 7.9 %collective-permute-start = (bf16[128,576]{1,0:T(8,128)(2,1)}, bf16[128,576]{1,0:T(8,128)(2,1)}, u32[]{:S(2)}, u32[]{:S(2)}) collective-permute-start(bf16[128,576]{1,0:T(8,128)(2,1)} %get-tuple-element.68), channel_id=1, source_target_pairs={{8,0},{16,8},{24,16},{9,1},{17,9},{25,17},{10,2},{18,10},{26,18},{... | collective-permute-start | bytes 442376 | tf_op jit(solution)/shard_map/ppermute | solution.py:14
  60.2 0.7 copy-start.5
  61.0 4.8 %collective-permute-start.3 = (bf16[2,2,16,576]{3,2,1,0:T(8,128)(2,1)S(1)}, bf16[2,2,16,576]{3,2,1,0:T(8,128)(2,1)S(1)}, u32[]{:S(2)}, u32[]{:S(2)}) collective-permute-start(bf16[2,2,16,576]{3,2,1,0:T(8,128)(2,1)S(1)} %bitcast_convert_fusion.1), channel_id=1, source_target_pairs={{0,1},{1,0},{2,3},{3,2},{4,5},{5,4},{6,7},{7,6},{8,9},{9,8},{10,11... | collective-permute-start | bytes 221192 | tf_op jit(solution)/shard_map/ppermute | solution.py:31
  66.7 4.1 %collective-permute-start.4 = (bf16[2,16,576]{2,1,0:T(8,128)(2,1)S(1)}, bf16[2,16,576]{2,1,0:T(8,128)(2,1)S(1)}, u32[]{:S(2)}, u32[]{:S(2)}) collective-permute-start(bf16[2,16,576]{2,1,0:T(8,128)(2,1)S(1)} %bitcast_convert_fusion.2), channel_id=1, source_target_pairs={{0,2},{1,3},{2,0},{3,1},{4,6},{5,7},{6,4},{7,5},{8,10},{9,11},{10,... | collective-permute-start | bytes 110600 | tf_op jit(solution)/shard_map/ppermute | solution.py:31
  70.8 4.7 %collective-permute-start.5 = (bf16[16,576]{1,0:T(8,128)(2,1)S(1)}, bf16[16,576]{1,0:T(8,128)(2,1)S(1)}, u32[]{:S(2)}, u32[]{:S(2)}) collective-permute-start(bf16[16,576]{1,0:T(8,128)(2,1)S(1)} %bitcast_convert_fusion.3), channel_id=1, source_target_pairs={{0,4},{1,5},{2,6},{3,7},{4,0},{5,1},{6,2},{7,3},{8,12},{9,13},{10,... | collective-permute-start | bytes 55304 | tf_op jit(solution)/shard_map/ppermute | solution.py:31
  75.6 4.9 %collective-permute-start.6 = (bf16[16,576]{1,0:T(8,128)(2,1)S(1)}, bf16[16,576]{1,0:T(8,128)(2,1)S(1)}, u32[]{:S(2)}, u32[]{:S(2)}) collective-permute-start(bf16[16,576]{1,0:T(8,128)(2,1)S(1)} %fusion.90), channel_id=1, source_target_pairs={{0,4},{1,5},{2,6},{3,7},{4,0},{5,1},{6,2},{7,3},{8,12},{9,13},{10,... | collective-permute-start | bytes 55304 | tf_op jit(solution)/shard_map/ppermute | solution.py:38
  80.4 5.7 %collective-permute-start.7 = (bf16[2,16,576]{2,1,0:T(8,128)(2,1)S(1)}, bf16[2,16,576]{2,1,0:T(8,128)(2,1)S(1)}, u32[]{:S(2)}, u32[]{:S(2)}) collective-permute-start(bf16[2,16,576]{2,1,0:T(8,128)(2,1)S(1)} %pad_maximum_fusion.3), channel_id=1, source_target_pairs={{0,2},{1,3},{2,0},{3,1},{4,6},{5,7},{6,4},{7,5},{8,10},{9,11},{10,... | collective-permute-start | bytes 110600 | tf_op jit(solution)/shard_map/ppermute | solution.py:38
  86.2 13.4 %collective-permute-start.8 = (bf16[2,2,16,576]{3,2,0,1:T(8,128)(2,1)S(1)}, bf16[2,2,16,576]{3,2,0,1:T(8,128)(2,1)S(1)}, u32[]{:S(2)}, u32[]{:S(2)}) collective-permute-start(bf16[2,2,16,576]{3,2,0,1:T(8,128)(2,1)S(1)} %pad_maximum_fusion.2), channel_id=1, source_target_pairs={{0,1},{1,0},{2,3},{3,2},{4,5},{5,4},{6,7},{7,6},{8,9},{9,8},{10,11... | collective-permute-start | bytes 221192 | tf_op jit(solution)/shard_map/ppermute | solution.py:38
where the time goes:
time: 102 us; the launch traced here: 101 us
  matrix products  33.1 us (32%)
  local copies, waits for them, and re-layouts  17.7 us (17%)
  waiting for transfers between devices  16.3 us (16%)
  starting transfers between devices  15.8 us (15%)
  blocking collectives  9.33 us (9%)
  other arithmetic  8.02 us (8%)
    unnamed x17, local copies, waits for them, and re-layouts  16.9 us
    all_gather x1, blocking collectives, body(): whole_keys = lax.all_gather(local_keys, 'ctx', axis=0, tiled=True)  9.33 us
    ppermute x3, waiting for transfers between devices, halving_sum_ep(): got = lax.ppermute(sent, 'ep', [(i, i ^ 1 << k) for i in range(n_ep)])  7.69 us
    dot_general x1, matrix products, body(): jnp.einsum('shtj,sthd->jd', rounded_weights, output_grad, preferred_eleme...  6.77 us
    ppermute x3, waiting for transfers between devices, causal_reduce_ctx(): lax.ppermute(sent, 'ctx', [(i, i - shift) for i in range(shift, n_ctx)])  6.4 us
    ppermute x3, starting transfers between devices, halving_sum_ep(): got = lax.ppermute(sent, 'ep', [(i, i ^ 1 << k) for i in range(n_ep)])  5.88 us
    ppermute x3, starting transfers between devices, halving_sum_ep(): got = lax.ppermute(whole, 'ep', [(i, i ^ 1 << k) for i in range(n_ep)])  5.79 us
    dot_general x1, matrix products, body(): jnp.einsum('sthd,sjd->shtj', output_grad, whole_latent, preferred_element...  4.7 us
  transfers between devices with their start and end apart: 9, of which 6 were waited for; matrix products, arithmetic and copies ran while one was open for 16% of the time, Pallas kernels for 0%

commit v1 on v0

--- a/solution.py
+++ b/solution.py
@@ -48,7 +48,21 @@
     block_len = query_latent.shape[1]
     kvr = key_latent.shape[2]
     local_keys = jnp.concatenate([key_latent[0], key_rope[0].T], axis=1)
-    whole_keys = lax.all_gather(local_keys, "ctx", axis=0, tiled=True)
+    ways, here_2, lap = (lax.axis_size("ctx"), lax.axis_index("ctx"), local_keys.shape[0])
+    lengths = [n * ways if d == 0 else n for d, n in enumerate(local_keys.shape)]
+    full = lax.dynamic_update_slice_in_dim(
+        jnp.zeros(lengths, local_keys.dtype), local_keys, here_2 * lap, axis=0
+    )
+    going_up = going_down = local_keys
+    for far in range(1, ways // 2 + 1):
+        going_up = lax.ppermute(going_up, "ctx", [(d, (d + 1) % ways) for d in range(ways)])
+        full = lax.dynamic_update_slice_in_dim(full, going_up, (here_2 - far) % ways * lap, axis=0)
+        if 2 * far < ways:
+            going_down = lax.ppermute(going_down, "ctx", [(d, (d - 1) % ways) for d in range(ways)])
+            full = lax.dynamic_update_slice_in_dim(
+                full, going_down, (here_2 + far) % ways * lap, axis=0
+            )
+    whole_keys = full
     whole_latent = whole_keys[None, :, :kvr]
     whole_rope = whole_keys[:, kvr:].T[None]
     length = whole_latent.shape[1]

time: 102 us -> 96.5 us (0.946)
  blocking collectives: 9.33 us -> 0 us
  matrix products: 33.1 us -> 25.7 us
  waiting for transfers between devices: 16.3 us -> 23 us
  starting transfers between devices: 15.8 us -> 19.8 us
    all_gather x1 -> x0, blocking collectives: 9.33 us -> none  [body(): whole_keys = lax.all_gather(local_keys, 'ctx', axis=0, tiled=True)]
    ppermute x0 -> x3, waiting for transfers between devices: none -> 5.89 us  [the longest x2 5.89 us: body(): lax.ppermute(going_up, 'ctx', [(d, (d + 1) % ways) for d in range(ways)])]
    ppermute x0 -> x3, starting transfers between devices: none -> 4.1 us  [the longest x2 2.11 us: body(): lax.ppermute(going_up, 'ctx', [(d, (d + 1) % ways) for d in range(ways)])]
    dot_general x1, matrix products: 4.44 us -> 2.57 us  [body(): jnp.einsum('shtj,sthd->jd', score_grad, query_latent, preferred_element_t...]
    dot_general x1, matrix products: 2.8 us -> 1.21 us  [body(): jnp.einsum('shtj,sdj->shdt', score_grad, whole_rope, preferred_element_ty...]
    dot_general x1, matrix products: 2.34 us -> 0.75 us  [body(): jnp.einsum('shtj,shdt->jd', score_grad, query_rope, preferred_element_typ...]
    dot_general x1, matrix products: 4.7 us -> 3.37 us  [body(): jnp.einsum('sthd,sjd->shtj', output_grad, whole_latent, preferred_element...]
    unnamed x17 -> x21, local copies, waits for them, and re-layouts: 16.9 us -> 17.5 us
  transfers between devices with their start and end apart: 9 -> 12, of which waited for: 6 -> 8; matrix products, arithmetic and copies ran while one was open for 16% -> 15% of each run, Pallas kernels for 0% -> 0%
where the time goes in v1:
time: 96.5 us; the launch traced here: 96 us
  matrix products  25.7 us (27%)
  waiting for transfers between devices  23 us (24%)
  starting transfers between devices  19.8 us (21%)
  local copies, waits for them, and re-layouts  18.4 us (19%)
  other arithmetic  8.05 us (8%)
  between operations  0.97 us (1%)
    unnamed x21, local copies, waits for them, and re-layouts  17.5 us
    ppermute x3, waiting for transfers between devices, halving_sum_ep(): got = lax.ppermute(sent, 'ep', [(i, i ^ 1 << k) for i in range(n_ep)])  7.76 us
    ppermute x3, waiting for transfers between devices, causal_reduce_ctx(): lax.ppermute(sent, 'ctx', [(i, i - shift) for i in range(shift, n_ctx)])  7.11 us
    ppermute x3, starting transfers between devices, halving_sum_ep(): got = lax.ppermute(sent, 'ep', [(i, i ^ 1 << k) for i in range(n_ep)])  5.91 us
    ppermute x2, waiting for transfers between devices, body(): lax.ppermute(going_up, 'ctx', [(d, (d + 1) % ways) for d in range(ways)])  5.89 us
    dot_general x1, matrix products, body(): jnp.einsum('shtj,sthd->jd', rounded_weights, output_grad, preferred_eleme...  5.8 us
    ppermute x3, starting transfers between devices, halving_sum_ep(): got = lax.ppermute(whole, 'ep', [(i, i ^ 1 << k) for i in range(n_ep)])  5.74 us
    dot_general x1, matrix products, body(): jnp.einsum('shtj,sjd->sthd', score_grad, whole_latent, preferred_element_...  4.21 us
  transfers between devices with their start and end apart: 12, of which 8 were waited for; matrix products, arithmetic and copies ran while one was open for 15% of the time, Pallas kernels for 0%

profile of v1, /device:TPU:0, one launch (start us, length us, event | category | flops | bytes accessed | tf_op | source)
XLA Modules:
  0.0 96.0 jit_solution(1523778104082245231)
XLA Ops:
  3.1 2.0 %collective-permute-start.1 = (bf16[128,576]{1,0:T(8,128)(2,1)S(1)}, bf16[128,576]{1,0:T(8,128)(2,1)S(1)}, u32[]{:S(2)}, u32[]{:S(2)}) collective-permute-start(bf16[128,576]{1,0:T(8,128)(2,1)S(1)} %get-tuple-element.73), channel_id=1, source_target_pairs={{0,24},{8,0},{16,8},{24,16},{1,25},{9,1},{17,9},{25,17},{2,26},{10... | collective-permute-start | bytes 442376 | tf_op jit(solution)/shard_map/ppermute | solution.py:61
  5.3 2.8 %collective-permute-done = bf16[128,576]{1,0:T(8,128)(2,1)S(1)} collective-permute-done((bf16[128,576]{1,0:T(8,128)(2,1)S(1)}, bf16[128,576]{1,0:T(8,128)(2,1)S(1)}, u32[]{:S(2)}, u32[]{:S(2)}) %collective-permute-start) | collective-permute-done | bytes 147488 | tf_op jit(solution)/shard_map/ppermute | solution.py:58
  8.1 1.6 %collective-permute-start.2 = (bf16[128,576]{1,0:T(8,128)(2,1)S(1)}, bf16[128,576]{1,0:T(8,128)(2,1)S(1)}, u32[]{:S(2)}, u32[]{:S(2)}) collective-permute-start(bf16[128,576]{1,0:T(8,128)(2,1)S(1)} %collective-permute-done), channel_id=1, source_target_pairs={{0,8},{8,16},{16,24},{24,0},{1,9},{9,17},{17,25},{25,1},{2,10},{10... | collective-permute-start | bytes 442376 | tf_op jit(solution)/shard_map/ppermute | solution.py:58
  9.8 3.1 %collective-permute-done.2 = bf16[128,576]{1,0:T(8,128)(2,1)S(1)} collective-permute-done((bf16[128,576]{1,0:T(8,128)(2,1)S(1)}, bf16[128,576]{1,0:T(8,128)(2,1)S(1)}, u32[]{:S(2)}, u32[]{:S(2)}) %collective-permute-start.2) | collective-permute-done | bytes 147488 | tf_op jit(solution)/shard_map/ppermute | solution.py:58
  12.9 2.8 %fusion.23 = f32[512,128,16]{1,0,2:T(8,128)S(1)} fusion(bf16[128,16,512]{2,1,0:T(8,128)(2,1)S(1)} %bitcast.189, bf16[512,576]{1,0:T(8,128)(2,1)S(1)} %constant_dynamic-update-slice_fusion), kind=kOutput, calls=%fused_computation.27 | convolution fusion | flops 1073741824 | bytes 6815744 | tf_op jit(solution)/shard_map/sthd,sjd->shtj/dot_general | solution.py:72
  17.2 4.1 %bitcast_convert_fusion = (f32[16,128,512]{1,2,0:T(8,128)}, bf16[512,16,128]{2,0,1:T(8,128)(2,1)}) fusion(f32[16,128]{1,0:T(8,128)S(1)} %fusion.5, f32[1,16,128,512]{2,3,1,0:T(8,128)S(1)} %get-tuple-element.80, f32[16,128]{1,0:T(8,128)S(1)} %get-tuple-element.79, bf16[512,576]{1,0:T(8,128)(2,1)S(1)} %constant_dynamic-update-slice_fusion), kind=kOutput, calls=%fused_computation.18 | convolution fusion | flops 1078984704 | bytes 11026432 | tf_op jit(solution)/shard_map/shtj,sjd->sthd/dot_general | solution.py:83
  21.3 5.5 %copy.81 = f32[16,128,512]{2,0,1:T(8,128)} copy(f32[16,128,512]{1,2,0:T(8,128)} %get-tuple-element.81) | data formatting | bytes 8388608
  26.8 3.3 %multiply_reduce_fusion = f32[16,128]{0,1:T(8,128)S(1)} fusion(f32[16,128,512]{2,0,1:T(8,128)} %copy.81, bf16[1,128,16,512]{3,2,1,0:T(8,128)(2,1)} %param.17), kind=kLoop, calls=%fused_computation.6 | loop fusion | flops 3143680 | bytes 6299648
  30.2 5.8 %fusion.28 = f32[512,512]{1,0:T(8,128)S(1)} fusion(bf16[128,16,512]{2,1,0:T(8,128)(2,1)} %bitcast.191, f32[16,128]{1,0:T(8,128)S(1)} %fusion.5, f32[1,16,128,512]{2,3,1,0:T(8,128)} %copy-done.1, f32[16,128]{1,0:T(8,128)S(1)} %get-tuple-element.79), kind=kOutput, calls=%fused_computation.30 | convolution fusion | flops 1076887552 | bytes 7356416 | tf_op jit(solution)/shard_map/shtj,sthd->jd/dot_general | solution.py:104
  36.0 3.4 %fusion.1 = bf16[1,16,128,512]{2,3,1,0:T(8,128)(2,1)S(1)} fusion(f32[16,128]{1,0:T(8,128)S(1)} %copy.82, bf16[128,16,512]{2,1,0:T(8,128)(2,1)S(1)} %bitcast.192, f32[16,128]{1,0:T(8,128)S(1)} %fusion.5, f32[1,16,128,512]{2,3,1,0:T(8,128)S(1)} %copy-done.2, f32[16,128]{1,0:T(8,128)S(1)} %get-tuple-element.79, ...), kind=kOutput, calls=%fused_computation.2 | convolution fusion | flops 1078984704 | bytes 8937472 | tf_op jit(solution)/shard_map/sthd,sjd->shtj/dot_general | solution.py:89
  40.7 2.6 %fusion.48 = bf16[512,512]{1,0:T(8,128)(2,1)S(1)} fusion(f32[512,512]{1,0:T(8,128)S(1)} %fusion.28, bf16[128,16,512]{2,1,0:T(8,128)(2,1)S(1)} %bitcast.190, bf16[1,16,128,512]{2,3,1,0:T(8,128)(2,1)S(1)} %fusion.1), kind=kOutput, calls=%fused_computation.34 | convolution fusion | flops 1074528256 | bytes 5767168 | tf_op jit(solution)/shard_map/shtj,sthd->jd/dot_general | solution.py:101
  48.4 2.8 %collective-permute-done.5 = bf16[128,576]{1,0:T(8,128)(2,1)} collective-permute-done((bf16[128,576]{1,0:T(8,128)(2,1)}, bf16[128,576]{1,0:T(8,128)(2,1)}, u32[]{:S(2)}, u32[]{:S(2)}) %collective-permute-start.5) | collective-permute-done | bytes 147488 | tf_op jit(solution)/shard_map/ppermute | solution.py:14
  51.2 4.3 %collective-permute-done.4 = bf16[128,576]{1,0:T(8,128)(2,1)} collective-permute-done((bf16[128,576]{1,0:T(8,128)(2,1)}, bf16[128,576]{1,0:T(8,128)(2,1)}, u32[]{:S(2)}, u32[]{:S(2)}) %collective-permute-start.4) | collective-permute-done | bytes 147488 | tf_op jit(solution)/shard_map/ppermute | solution.py:14
  57.4 1.7 %collective-permute-start.6 = (bf16[2,2,16,576]{3,2,1,0:T(8,128)(2,1)S(1)}, bf16[2,2,16,576]{3,2,1,0:T(8,128)(2,1)S(1)}, u32[]{:S(2)}, u32[]{:S(2)}) collective-permute-start(bf16[2,2,16,576]{3,2,1,0:T(8,128)(2,1)S(1)} %bitcast_convert_fusion.1), channel_id=1, source_target_pairs={{0,1},{1,0},{2,3},{3,2},{4,5},{5,4},{6,7},{7,6},{8,9},{9,8},{10,11... | collective-permute-start | bytes 221192 | tf_op jit(solution)/shard_map/ppermute | solution.py:31
  59.1 3.2 %collective-permute-done.6 = bf16[2,2,16,576]{3,2,1,0:T(8,128)(2,1)S(1)} collective-permute-done((bf16[2,2,16,576]{3,2,1,0:T(8,128)(2,1)S(1)}, bf16[2,2,16,576]{3,2,1,0:T(8,128)(2,1)S(1)}, u32[]{:S(2)}, u32[]{:S(2)}) %collective-permute-start.6) | collective-permute-done | bytes 73760 | tf_op jit(solution)/shard_map/ppermute | solution.py:31
  63.2 1.6 %collective-permute-start.7 = (bf16[2,16,576]{2,1,0:T(8,128)(2,1)S(1)}, bf16[2,16,576]{2,1,0:T(8,128)(2,1)S(1)}, u32[]{:S(2)}, u32[]{:S(2)}) collective-permute-start(bf16[2,16,576]{2,1,0:T(8,128)(2,1)S(1)} %bitcast_convert_fusion.2), channel_id=1, source_target_pairs={{0,2},{1,3},{2,0},{3,1},{4,6},{5,7},{6,4},{7,5},{8,10},{9,11},{10,... | collective-permute-start | bytes 110600 | tf_op jit(solution)/shard_map/ppermute | solution.py:31
  64.8 2.5 %collective-permute-done.7 = bf16[2,16,576]{2,1,0:T(8,128)(2,1)S(1)} collective-permute-done((bf16[2,16,576]{2,1,0:T(8,128)(2,1)S(1)}, bf16[2,16,576]{2,1,0:T(8,128)(2,1)S(1)}, u32[]{:S(2)}, u32[]{:S(2)}) %collective-permute-start.7) | collective-permute-done | bytes 36896 | tf_op jit(solution)/shard_map/ppermute | solution.py:31
  67.3 2.6 %collective-permute-start.8 = (bf16[16,576]{1,0:T(8,128)(2,1)S(1)}, bf16[16,576]{1,0:T(8,128)(2,1)S(1)}, u32[]{:S(2)}, u32[]{:S(2)}) collective-permute-start(bf16[16,576]{1,0:T(8,128)(2,1)S(1)} %bitcast_convert_fusion.3), channel_id=1, source_target_pairs={{0,4},{1,5},{2,6},{3,7},{4,0},{5,1},{6,2},{7,3},{8,12},{9,13},{10,... | collective-permute-start | bytes 55304 | tf_op jit(solution)/shard_map/ppermute | solution.py:31
  70.0 2.1 %collective-permute-done.8 = bf16[16,576]{1,0:T(8,128)(2,1)S(1)} collective-permute-done((bf16[16,576]{1,0:T(8,128)(2,1)S(1)}, bf16[16,576]{1,0:T(8,128)(2,1)S(1)}, u32[]{:S(2)}, u32[]{:S(2)}) %collective-permute-start.8) | collective-permute-done | bytes 18464 | tf_op jit(solution)/shard_map/ppermute | solution.py:31
  72.1 2.6 %collective-permute-start.9 = (bf16[16,576]{1,0:T(8,128)(2,1)S(1)}, bf16[16,576]{1,0:T(8,128)(2,1)S(1)}, u32[]{:S(2)}, u32[]{:S(2)}) collective-permute-start(bf16[16,576]{1,0:T(8,128)(2,1)S(1)} %fusion.90), channel_id=1, source_target_pairs={{0,4},{1,5},{2,6},{3,7},{4,0},{5,1},{6,2},{7,3},{8,12},{9,13},{10,... | collective-permute-start | bytes 55304 | tf_op jit(solution)/shard_map/ppermute | solution.py:38
  74.7 2.2 %collective-permute-done.9 = bf16[16,576]{1,0:T(8,128)(2,1)S(1)} collective-permute-done((bf16[16,576]{1,0:T(8,128)(2,1)S(1)}, bf16[16,576]{1,0:T(8,128)(2,1)S(1)}, u32[]{:S(2)}, u32[]{:S(2)}) %collective-permute-start.9) | collective-permute-done | bytes 18464 | tf_op jit(solution)/shard_map/ppermute | solution.py:38
  78.5 4.2 %fusion.25 = bf16[1,128,16,512]{1,3,2,0:T(8,128)(2,1)} fusion(bf16[1,16,128,512]{2,3,1,0:T(8,128)(2,1)} %copy-done.3, bf16[512,576]{1,0:T(8,128)(2,1)S(1)} %constant_dynamic-update-slice_fusion), kind=kOutput, calls=%fused_computation.29 | convolution fusion | flops 1075838976 | bytes 4718592 | tf_op jit(solution)/shard_map/shtj,sjd->sthd/dot_general | solution.py:95
  85.6 4.5 %copy.70 = bf16[1,128,16,512]{3,2,1,0:T(8,128)(2,1)} copy(bf16[1,128,16,512]{1,3,2,0:T(8,128)(2,1)} %bitcast.193) | data formatting | bytes 4194304
  90.0 4.5 %copy.71 = bf16[1,128,16,512]{3,2,1,0:T(8,128)(2,1)} copy(bf16[1,128,16,512]{1,3,2,0:T(8,128)(2,1)} %fusion.25) | data formatting | bytes 4194304
  (58 shorter events, 19.2 us)
Async XLA Ops:
  0.6 12.2 %copy-start = (bf16[1,128,16,512]{3,2,1,0:T(8,128)(2,1)S(1)}, bf16[1,128,16,512]{3,2,1,0:T(8,128)(2,1)}, u32[]{:S(2)}) copy-start(bf16[1,128,16,512]{3,2,1,0:T(8,128)(2,1)} %param.13) | copy-start | bytes 6291460
  2.6 5.4 %collective-permute-start = (bf16[128,576]{1,0:T(8,128)(2,1)S(1)}, bf16[128,576]{1,0:T(8,128)(2,1)S(1)}, u32[]{:S(2)}, u32[]{:S(2)}) collective-permute-start(bf16[128,576]{1,0:T(8,128)(2,1)S(1)} %get-tuple-element.73), channel_id=1, source_target_pairs={{0,8},{8,16},{16,24},{24,0},{1,9},{9,17},{17,25},{25,1},{2,10},{10... | collective-permute-start | bytes 442376 | tf_op jit(solution)/shard_map/ppermute | solution.py:58
  3.1 6.6 %collective-permute-start.1 = (bf16[128,576]{1,0:T(8,128)(2,1)S(1)}, bf16[128,576]{1,0:T(8,128)(2,1)S(1)}, u32[]{:S(2)}, u32[]{:S(2)}) collective-permute-start(bf16[128,576]{1,0:T(8,128)(2,1)S(1)} %get-tuple-element.73), channel_id=1, source_target_pairs={{0,24},{8,0},{16,8},{24,16},{1,25},{9,1},{17,9},{25,17},{2,26},{10... | collective-permute-start | bytes 442376 | tf_op jit(solution)/shard_map/ppermute | solution.py:61
  8.1 4.7 %collective-permute-start.2 = (bf16[128,576]{1,0:T(8,128)(2,1)S(1)}, bf16[128,576]{1,0:T(8,128)(2,1)S(1)}, u32[]{:S(2)}, u32[]{:S(2)}) collective-permute-start(bf16[128,576]{1,0:T(8,128)(2,1)S(1)} %collective-permute-done), channel_id=1, source_target_pairs={{0,8},{8,16},{16,24},{24,0},{1,9},{9,17},{17,25},{25,1},{2,10},{10... | collective-permute-start | bytes 442376 | tf_op jit(solution)/shard_map/ppermute | solution.py:58
  12.9 2.8 %copy-start.6 = (bf16[1,16,64,128]{3,2,1,0:T(8,128)(2,1)S(1)}, bf16[1,16,64,128]{3,2,1,0:T(8,128)(2,1)}, u32[]{:S(2)}) copy-start(bf16[1,16,64,128]{3,2,1,0:T(8,128)(2,1)} %param.14) | copy-start | bytes 786436
  16.6 4.7 %copy-start.1 = (f32[1,16,128,512]{2,3,1,0:T(8,128)}, f32[1,16,128,512]{2,3,1,0:T(8,128)S(1)}, u32[]{:S(2)}) copy-start(f32[1,16,128,512]{2,3,1,0:T(8,128)S(1)} %get-tuple-element.80) | copy-start | bytes 12582916
  30.2 5.8 %copy-start.2 = (f32[1,16,128,512]{2,3,1,0:T(8,128)S(1)}, f32[1,16,128,512]{2,3,1,0:T(8,128)}, u32[]{:S(2)}) copy-start(f32[1,16,128,512]{2,3,1,0:T(8,128)} %copy-done.1) | copy-start | bytes 12582916
  30.2 5.8 %copy-start.5 = (bf16[1,128,16,512]{3,2,1,0:T(8,128)(2,1)S(1)}, bf16[1,128,16,512]{3,2,1,0:T(8,128)(2,1)}, u32[]{:S(2)}) copy-start(bf16[1,128,16,512]{3,2,1,0:T(8,128)(2,1)} %param.17) | copy-start | bytes 6291460
  39.4 1.3 %copy-start.3 = (bf16[1,16,128,512]{2,3,1,0:T(8,128)(2,1)}, bf16[1,16,128,512]{2,3,1,0:T(8,128)(2,1)S(1)}, u32[]{:S(2)}) copy-start(bf16[1,16,128,512]{2,3,1,0:T(8,128)(2,1)S(1)} %fusion.1) | copy-start | bytes 6291460
  44.3 6.9 %collective-permute-start.5 = (bf16[128,576]{1,0:T(8,128)(2,1)}, bf16[128,576]{1,0:T(8,128)(2,1)}, u32[]{:S(2)}, u32[]{:S(2)}) collective-permute-start(bf16[128,576]{1,0:T(8,128)(2,1)} %get-tuple-element.70), channel_id=1, source_target_pairs={{24,0},{25,1},{26,2},{27,3},{28,4},{29,5},{30,6},{31,7}} | collective-permute-start | bytes 442376 | tf_op jit(solution)/shard_map/ppermute | solution.py:14
  45.6 9.9 %collective-permute-start.4 = (bf16[128,576]{1,0:T(8,128)(2,1)}, bf16[128,576]{1,0:T(8,128)(2,1)}, u32[]{:S(2)}, u32[]{:S(2)}) collective-permute-start(bf16[128,576]{1,0:T(8,128)(2,1)} %get-tuple-element.69), channel_id=1, source_target_pairs={{16,0},{24,8},{17,1},{25,9},{18,2},{26,10},{19,3},{27,11},{20,4},{... | collective-permute-start | bytes 442376 | tf_op jit(solution)/shard_map/ppermute | solution.py:14
  46.9 8.7 %collective-permute-start.3 = (bf16[128,576]{1,0:T(8,128)(2,1)}, bf16[128,576]{1,0:T(8,128)(2,1)}, u32[]{:S(2)}, u32[]{:S(2)}) collective-permute-start(bf16[128,576]{1,0:T(8,128)(2,1)} %get-tuple-element.68), channel_id=1, source_target_pairs={{8,0},{16,8},{24,16},{9,1},{17,9},{25,17},{10,2},{18,10},{26,18},{... | collective-permute-start | bytes 442376 | tf_op jit(solution)/shard_map/ppermute | solution.py:14
  56.7 0.7 copy-start.7
  57.4 4.8 %collective-permute-start.6 = (bf16[2,2,16,576]{3,2,1,0:T(8,128)(2,1)S(1)}, bf16[2,2,16,576]{3,2,1,0:T(8,128)(2,1)S(1)}, u32[]{:S(2)}, u32[]{:S(2)}) collective-permute-start(bf16[2,2,16,576]{3,2,1,0:T(8,128)(2,1)S(1)} %bitcast_convert_fusion.1), channel_id=1, source_target_pairs={{0,1},{1,0},{2,3},{3,2},{4,5},{5,4},{6,7},{7,6},{8,9},{9,8},{10,11... | collective-permute-start | bytes 221192 | tf_op jit(solution)/shard_map/ppermute | solution.py:31
  63.2 4.1 %collective-permute-start.7 = (bf16[2,16,576]{2,1,0:T(8,128)(2,1)S(1)}, bf16[2,16,576]{2,1,0:T(8,128)(2,1)S(1)}, u32[]{:S(2)}, u32[]{:S(2)}) collective-permute-start(bf16[2,16,576]{2,1,0:T(8,128)(2,1)S(1)} %bitcast_convert_fusion.2), channel_id=1, source_target_pairs={{0,2},{1,3},{2,0},{3,1},{4,6},{5,7},{6,4},{7,5},{8,10},{9,11},{10,... | collective-permute-start | bytes 110600 | tf_op jit(solution)/shard_map/ppermute | solution.py:31
  67.3 4.7 %collective-permute-start.8 = (bf16[16,576]{1,0:T(8,128)(2,1)S(1)}, bf16[16,576]{1,0:T(8,128)(2,1)S(1)}, u32[]{:S(2)}, u32[]{:S(2)}) collective-permute-start(bf16[16,576]{1,0:T(8,128)(2,1)S(1)} %bitcast_convert_fusion.3), channel_id=1, source_target_pairs={{0,4},{1,5},{2,6},{3,7},{4,0},{5,1},{6,2},{7,3},{8,12},{9,13},{10,... | collective-permute-start | bytes 55304 | tf_op jit(solution)/shard_map/ppermute | solution.py:31
  72.1 4.9 %collective-permute-start.9 = (bf16[16,576]{1,0:T(8,128)(2,1)S(1)}, bf16[16,576]{1,0:T(8,128)(2,1)S(1)}, u32[]{:S(2)}, u32[]{:S(2)}) collective-permute-start(bf16[16,576]{1,0:T(8,128)(2,1)S(1)} %fusion.90), channel_id=1, source_target_pairs={{0,4},{1,5},{2,6},{3,7},{4,0},{5,1},{6,2},{7,3},{8,12},{9,13},{10,... | collective-permute-start | bytes 55304 | tf_op jit(solution)/shard_map/ppermute | solution.py:38
  74.7 9.6 %copy-start.4 = (bf16[1,16,128,512]{2,3,1,0:T(8,128)(2,1)S(1)}, bf16[1,16,128,512]{2,3,1,0:T(8,128)(2,1)}, u32[]{:S(2)}) copy-start(bf16[1,16,128,512]{2,3,1,0:T(8,128)(2,1)} %copy-done.3) | copy-start | bytes 6291460
  77.0 5.7 %collective-permute-start.10 = (bf16[2,16,576]{2,1,0:T(8,128)(2,1)S(1)}, bf16[2,16,576]{2,1,0:T(8,128)(2,1)S(1)}, u32[]{:S(2)}, u32[]{:S(2)}) collective-permute-start(bf16[2,16,576]{2,1,0:T(8,128)(2,1)S(1)} %pad_maximum_fusion.3), channel_id=1, source_target_pairs={{0,2},{1,3},{2,0},{3,1},{4,6},{5,7},{6,4},{7,5},{8,10},{9,11},{10,... | collective-permute-start | bytes 110600 | tf_op jit(solution)/shard_map/ppermute | solution.py:38
  82.7 11.8 %collective-permute-start.11 = (bf16[2,2,16,576]{3,2,0,1:T(8,128)(2,1)S(1)}, bf16[2,2,16,576]{3,2,0,1:T(8,128)(2,1)S(1)}, u32[]{:S(2)}, u32[]{:S(2)}) collective-permute-start(bf16[2,2,16,576]{3,2,0,1:T(8,128)(2,1)S(1)} %pad_maximum_fusion.2), channel_id=1, source_target_pairs={{0,1},{1,0},{2,3},{3,2},{4,5},{5,4},{6,7},{7,6},{8,9},{9,8},{10,11... | collective-permute-start | bytes 221192 | tf_op jit(solution)/shard_map/ppermute | solution.py:38
